TPU v7x, 32 devices: a whole 2x2x4 slice. The times are simulated.
32 devices in a mesh: rep: 4 (over y, core), ep: 8 (over z, x).
Axes of the slice: x: 2, y: 2, z: 4, core: 2. Of those that a mesh axis runs over, the one named last changes fastest.
Arguments:
- tokens: bfloat16 [8192, 2048], P(('rep', 'ep')), may hold values from -6 to 6
- expert_ids: int32 [8192, 8], P(('rep', 'ep')), may hold values from 0 to 127, as said below
- gate_weights: float32 [8192, 8], P(('rep', 'ep')), may hold values from 0.25 to 1
- w_gate: bfloat16 [8, 768, 2048], P('ep'), may hold values from -0.125 to 0.125
- w_up: bfloat16 [8, 768, 2048], P('ep'), may hold values from -0.125 to 0.125
- w_down: bfloat16 [8, 768, 2048], P('ep'), may hold values from -0.21875 to 0.21875
- out_grad: bfloat16 [8192, 2048], P(('rep', 'ep')), may hold values from -6 to 6
Outputs:
- layer_out: bfloat16 [8192, 2048], P(('rep', 'ep'))
- tokens_grad: bfloat16 [8192, 2048], P(('rep', 'ep'))
- gates_grad: float32 [8192, 8], P(('rep', 'ep'))
- gate_w_grad: bfloat16 [8, 768, 2048], P('ep', 'rep')
- up_w_grad: bfloat16 [8, 768, 2048], P('ep', 'rep')
- down_w_grad: bfloat16 [8, 768, 2048], P('ep', 'rep')
Inputs may be any that keep to these rules, and one draw needn't show every extreme that they name: `expert_ids`: entry j of a row lies in [16 * j, 16 * j + 16); in the rows of one device no id below 8 appears more than 32 times, and some id below 8 appears exactly 32 times.
All inputs are finite; a program needn't handle non-finite values.
Results may differ from a plain program's by a relative error of at most 0.0065.
Values may be sent and summed in bfloat16 or wider, within the bound.
No kernel may reach another device: no remote copies, remote signals or barrier semaphores. Data moves between devices by JAX's collectives and lax.ppermute only.
A program may use at most 128 MiB of HBM per device.

v0:
```python
import jax
import jax.numpy as jnp
from jax import lax
from jax.sharding import PartitionSpec as P

STRIPE = 16


def silu_grad(value):
    sigmoid_value = jax.nn.sigmoid(value)
    return sigmoid_value * (1.0 + value * (1.0 - sigmoid_value))


def rows_times(left, right):
    return lax.dot_general(
        left, right, (((1,), (1,)), ((), ())), preferred_element_type=jnp.float32
    )


def inner_rows(left, right):
    return lax.dot_general(
        left, right, (((0,), (0,)), ((), ())), preferred_element_type=jnp.float32
    )


def matmul(left, right):
    return jnp.dot(left, right, preferred_element_type=jnp.float32)


def body(tokens, expert_ids, gate_weights, w_gate, w_up, w_down, out_grad):
    tok_count, feature_width = tokens.shape
    top_count = expert_ids.shape[1]
    experts = lax.axis_size("ep")
    per_pair = tok_count // 8
    total_slots = experts * per_pair
    live_cols = min(top_count, -(-experts // STRIPE))
    assigned = tok_count * live_cols
    flat_ids = expert_ids[:, :live_cols].reshape(-1)
    flat_gates = gate_weights[:, :live_cols].reshape(-1)
    live_mask = flat_ids < experts
    onehot = flat_ids[:, None] == jnp.arange(experts, dtype=jnp.int32)[None, :]
    position = jnp.arange(assigned, dtype=jnp.int32)
    earlier = (position[:, None] > position[None, :]).astype(jnp.bfloat16)
    before = matmul(earlier, onehot.astype(jnp.bfloat16))
    slot_rank = jnp.sum(jnp.where(onehot, before, 0.0), axis=1).astype(jnp.int32)
    slot_index = jnp.where(live_mask, flat_ids * per_pair + slot_rank, -1)
    slot_ids = jnp.arange(total_slots, dtype=jnp.int32)
    hit = slot_ids[:, None] == slot_index[None, :]
    slot_gate = jnp.sum(jnp.where(hit, flat_gates[None, :], 0.0), axis=1)
    pick = jnp.any(hit.reshape(total_slots, tok_count, live_cols), axis=2).astype(jnp.bfloat16)
    send_rows = matmul(pick, tokens).astype(jnp.bfloat16)
    grad_rows = matmul(pick, out_grad)
    scaled_grad = (slot_gate[:, None] * grad_rows).astype(jnp.bfloat16)

    def exchange(rows):
        return lax.all_to_all(
            rows.reshape(experts, per_pair, feature_width),
            "ep",
            split_axis=0,
            concat_axis=0,
            tiled=True,
        ).reshape(total_slots, feature_width)

    rows_in = exchange(send_rows)
    grad_in = exchange(scaled_grad)
    copies = lax.axis_size("rep")
    by_pieces = copies == 4

    def to_copy(values, step):
        return lax.ppermute(values, "rep", [(r, r ^ step) for r in range(copies)])

    if by_pieces:
        far_rows = to_copy(rows_in, 2)
        near_rows = to_copy(rows_in, 1)
    else:
        gathered_rows = lax.all_gather(rows_in, "rep", axis=0, tiled=True)
        gathered_grad = lax.all_gather(grad_in, "rep", axis=0, tiled=True)
    gate_mat = w_gate[0]
    up_mat = w_up[0]
    down_mat = w_down[0]
    gate_up_mat = jnp.concatenate([gate_mat, up_mat], axis=0)
    hidden_units = gate_mat.shape[0]
    pre_both_own = rows_times(rows_in, gate_up_mat)
    pre_gate = pre_both_own[:, :hidden_units]
    pre_up = pre_both_own[:, hidden_units:]
    activated = jax.nn.silu(pre_gate)
    hidden = (activated * pre_up).astype(jnp.bfloat16)
    expert_out = matmul(hidden, down_mat).astype(jnp.bfloat16)
    expert_out, grad_in = lax.optimization_barrier((expert_out, grad_in))
    returned = lax.all_to_all(
        expert_out.reshape(experts, per_pair, feature_width),
        "ep",
        split_axis=0,
        concat_axis=0,
        tiled=True,
    ).reshape(total_slots, feature_width)
    hidden_grad = rows_times(grad_in, down_mat)
    gate_pre_grad = (hidden_grad * pre_up * silu_grad(pre_gate)).astype(jnp.bfloat16)
    up_pre_grad = (hidden_grad * activated).astype(jnp.bfloat16)
    token_part = matmul(jnp.concatenate([gate_pre_grad, up_pre_grad], axis=1), gate_up_mat).astype(
        jnp.bfloat16
    )
    if by_pieces:
        token_part, grad_out = lax.optimization_barrier((token_part, grad_in))
        far_grad = to_copy(grad_out, 2)
        near_grad = to_copy(grad_out, 1)
    part_back = lax.all_to_all(
        token_part.reshape(experts, per_pair, feature_width),
        "ep",
        split_axis=0,
        concat_axis=0,
        tiled=True,
    ).reshape(total_slots, feature_width)
    if by_pieces:
        returned, near_rows, near_grad = lax.optimization_barrier((returned, near_rows, near_grad))
    slot_grid = slot_index.reshape(tok_count, live_cols)
    gate_grid = flat_gates.reshape(tok_count, live_cols)
    layer_sum = jnp.zeros((tok_count, feature_width), jnp.float32)
    gate_cols = []
    back_pick = jnp.zeros((tok_count, total_slots), jnp.bfloat16)
    for col in range(live_cols):
        col_pick = (slot_grid[:, col : col + 1] == slot_ids[None, :]).astype(jnp.bfloat16)
        back_pick = back_pick + col_pick
        out_rows = matmul(col_pick, returned)
        layer_sum = layer_sum + gate_grid[:, col : col + 1] * out_rows
        gate_cols.append(jnp.sum(out_grad.astype(jnp.float32) * out_rows, axis=1))
    if by_pieces:
        layer_sum, far_rows, far_grad = lax.optimization_barrier((layer_sum, far_rows, far_grad))
        pieces = [
            (rows_in, grad_in),
            (near_rows, near_grad),
            (far_rows, far_grad),
            (to_copy(far_rows, 1), to_copy(far_grad, 1)),
        ]
    else:
        pieces = [(gathered_rows, gathered_grad)]
    layer_out = layer_sum.astype(jnp.bfloat16)
    gate_cols.extend([jnp.zeros((tok_count,), jnp.float32)] * (top_count - live_cols))
    gates_grad = jnp.stack(gate_cols, axis=1)
    share = gate_mat.shape[0] // copies
    start = lax.axis_index("rep") * share
    gate_share = lax.dynamic_slice_in_dim(gate_mat, start, share, axis=0)
    up_share = lax.dynamic_slice_in_dim(up_mat, start, share, axis=0)
    down_share = lax.dynamic_slice_in_dim(down_mat, start, share, axis=0)
    both_sum = None
    down_sum = None
    stacked_share = jnp.concatenate([gate_share, up_share], axis=0)
    for rows_p, grad_p in pieces:
        pre_both = rows_times(rows_p, stacked_share)
        pre_gate_s = pre_both[:, :share]
        pre_up_s = pre_both[:, share:]
        activated_s = jax.nn.silu(pre_gate_s)
        hidden_s = (activated_s * pre_up_s).astype(jnp.bfloat16)
        hidden_grad_s = rows_times(grad_p, down_share)
        gate_pre_grad_s = (hidden_grad_s * pre_up_s * silu_grad(pre_gate_s)).astype(jnp.bfloat16)
        up_pre_grad_s = (hidden_grad_s * activated_s).astype(jnp.bfloat16)
        both_p = inner_rows(jnp.concatenate([gate_pre_grad_s, up_pre_grad_s], axis=1), rows_p)
        down_p = inner_rows(hidden_s, grad_p)
        both_sum = both_p if both_sum is None else both_sum + both_p
        down_sum = down_p if down_sum is None else down_sum + down_p
    gate_w_grad = both_sum[:share].astype(jnp.bfloat16)[None]
    up_w_grad = both_sum[share:].astype(jnp.bfloat16)[None]
    down_w_grad = down_sum.astype(jnp.bfloat16)[None]
    part_back, gate_w_grad, up_w_grad, down_w_grad = lax.optimization_barrier(
        (part_back, gate_w_grad, up_w_grad, down_w_grad)
    )
    tokens_grad = matmul(back_pick, part_back).astype(jnp.bfloat16)
    return (layer_out, tokens_grad, gates_grad, gate_w_grad, up_w_grad, down_w_grad)


def solution(mesh):
    return jax.shard_map(
        body,
        mesh=mesh,
        in_specs=(
            P(("rep", "ep"), None),
            P(("rep", "ep"), None),
            P(("rep", "ep"), None),
            P("ep", None, None),
            P("ep", None, None),
            P("ep", None, None),
            P(("rep", "ep"), None),
        ),
        out_specs=(
            P(("rep", "ep"), None),
            P(("rep", "ep"), None),
            P(("rep", "ep"), None),
            P("ep", "rep", None),
            P("ep", "rep", None),
            P("ep", "rep", None),
        ),
        check_vma=False,
    )
```

profile of v0, /device:TPU:0, one launch (start us, length us, event | category | flops | bytes accessed | tf_op | source)
XLA Modules:
  0.0 129.3 jit_solution(9352168649783690748)
XLA Ops:
  0.6 0.0 copy-start
  0.6 0.9 slice.45
  1.5 0.2 fusion.14
  1.7 2.6 %convolution_convert_fusion.1 = bf16[256,2048]{1,0:T(8,128)(2,1)} fusion(bf16[256,2048]{1,0:T(8,128)(2,1)} %param.7, s32[256]{0:T(256)S(1)} %compare_select_fusion.1), kind=kOutput, calls=%fused_computation.14 | convolution fusion | flops 269025280 | bytes 2098176 | tf_op jit(solution)/shard_map/dot_general | solution.py:27
  4.4 7.3 %all-to-all-start = ((bf16[8,32,2048]{2,1,0:T(8,128)(2,1)}), bf16[8,32,2048]{2,1,0:T(8,128)(2,1)}, u32[]{:S(2)}, u32[]{:S(2)}) async-start(bf16[8,32,2048]{2,1,0:T(8,128)(2,1)} %bitcast.75), calls=%async_computation | async-start | bytes 2097152 | tf_op jit(solution)/shard_map/all_to_all | solution.py:56
  11.6 0.7 slice.44
  12.3 0.1 select_reduce_fusion
  12.4 2.6 %fusion.6 = bf16[256,2048]{1,0:T(8,128)(2,1)} fusion(bf16[256,2048]{1,0:T(8,128)(2,1)} %param.13, f32[256]{0:T(256)S(1)} %select_reduce_fusion, s32[256]{0:T(256)S(1)} %compare_select_fusion.1), kind=kOutput, calls=%fused_computation.11 | convolution fusion | flops 269549568 | bytes 2099200 | tf_op jit(solution)/shard_map/dot_general | solution.py:27
  15.1 22.4 %all-to-all-done = bf16[8,32,2048]{2,1,0:T(8,128)(2,1)} async-done(((bf16[8,32,2048]{2,1,0:T(8,128)(2,1)}), bf16[8,32,2048]{2,1,0:T(8,128)(2,1)}, u32[]{:S(2)}, u32[]{:S(2)}) %all-to-all-start) | async-done | bytes 1048608 | tf_op jit(solution)/shard_map/all_to_all | solution.py:56
  37.5 4.3 %all-to-all-start.1 = ((bf16[8,32,2048]{2,1,0:T(8,128)(2,1)}), bf16[8,32,2048]{2,1,0:T(8,128)(2,1)}, u32[]{:S(2)}, u32[]{:S(2)}) async-start(bf16[8,32,2048]{2,1,0:T(8,128)(2,1)} %bitcast.74), calls=%async_computation.1 | async-start | bytes 2097152 | tf_op jit(solution)/shard_map/all_to_all | solution.py:56
  41.8 0.1 pad.1.clone
  41.9 0.1 pad.3.clone
  41.9 0.1 pad.2.clone
  42.0 0.9 compare_select_fusion
  42.9 2.8 %dynamic-slice_bitcast_fusion = (bf16[192,2048]{1,0:T(8,128)(2,1)}, bf16[192,2048]{1,0:T(8,128)(2,1)}) fusion(bf16[1,768,2048]{2,1,0:T(8,128)(2,1)} %param.11, s32[]{:T(128)S(6)} %select_n.28, bf16[1,768,2048]{2,1,0:T(8,128)(2,1)} %param.10), kind=kLoop, calls=%fused_computation.37 | loop fusion | bytes 3145732 | tf_op jit(solution)/shard_map/dynamic_slice | solution.py:143
  45.7 1.5 %collective-permute-start.2 = (bf16[256,2048]{1,0:T(8,128)(2,1)}, bf16[256,2048]{1,0:T(8,128)(2,1)}, u32[]{:S(2)}, u32[]{:S(2)}) collective-permute-start(bf16[256,2048]{1,0:T(8,128)(2,1)} %bitcast.5), channel_id=1, source_target_pairs={{0,16},{8,24},{16,0},{24,8},{1,17},{9,25},{17,1},{25,9},{2,18},{10... | collective-permute-start | bytes 3145736 | tf_op jit(solution)/shard_map/ppermute | solution.py:70
  47.2 0.0 collective-permute-start
  47.2 4.0 %fusion.1 = f32[256,1536]{1,0:T(8,128)S(1)} fusion(bf16[256,2048]{1,0:T(8,128)(2,1)} %bitcast.5, bf16[768,2048]{1,0:T(8,128)(2,1)S(1)} %bitcast.78, bf16[768,2048]{1,0:T(8,128)(2,1)} %bitcast.80), kind=kOutput, calls=%fused_computation.2 | convolution fusion | flops 1623195648 | bytes 8912896 | tf_op jit(solution)/shard_map/dot_general | solution.py:15
  51.2 1.2 copy-done.11
  52.4 2.0 %fusion.9 = bf16[256,2048]{1,0:T(8,128)(2,1)} fusion(bf16[1,768,2048]{2,1,0:T(8,128)(2,1)S(1)} %copy-done, f32[256,1536]{1,0:T(8,128)S(1)} %fusion.1), kind=kOutput, calls=%fused_computation.16 | convolution fusion | flops 807010304 | bytes 5767168 | tf_op jit(solution)/shard_map/dot_general | solution.py:27
  54.4 12.9 %all-to-all-done.1 = bf16[8,32,2048]{2,1,0:T(8,128)(2,1)} async-done(((bf16[8,32,2048]{2,1,0:T(8,128)(2,1)}), bf16[8,32,2048]{2,1,0:T(8,128)(2,1)}, u32[]{:S(2)}, u32[]{:S(2)}) %all-to-all-start.1) | async-done | bytes 1048608 | tf_op jit(solution)/shard_map/all_to_all | solution.py:56
  67.3 4.2 %all-to-all-start.2 = ((bf16[8,32,2048]{2,1,0:T(8,128)(2,1)}), bf16[8,32,2048]{2,1,0:T(8,128)(2,1)}, u32[]{:S(2)}, u32[]{:S(2)}) async-start(bf16[8,32,2048]{2,1,0:T(8,128)(2,1)} %bitcast.77), calls=%async_computation.2 | async-start | bytes 2097152 | tf_op jit(solution)/shard_map/all_to_all | solution.py:90
  71.6 0.0 copy-start.9
  71.6 0.0 copy-start.10
  71.6 3.0 %multiply_convert_fusion.1 = (bf16[256,768]{1,0:T(8,128)(2,1)S(1)}, bf16[256,768]{1,0:T(8,128)(2,1)S(1)}) fusion(f32[256,1536]{1,0:T(8,128)} %copy-done.11, bf16[256,2048]{1,0:T(8,128)(2,1)} %bitcast.10, bf16[1,768,2048]{2,1,0:T(8,128)(2,1)S(1)} %copy-done), kind=kOutput, calls=%fused_computation.40 | convolution fusion | flops 807862272 | bytes 6553600 | tf_op jit(solution)/shard_map/dot_general | solution.py:15
  74.7 0.6 copy-done.10
  75.2 2.8 %fusion.7 = bf16[256,2048]{1,0:T(8,128)(2,1)} fusion(bf16[768,2048]{1,0:T(8,128)(2,1)S(1)} %bitcast.79, bf16[768,2048]{1,0:T(8,128)(2,1)S(1)} %bitcast.81, bf16[256,768]{1,0:T(8,128)(2,1)S(1)} %get-tuple-element.35, bf16[256,768]{1,0:T(8,128)(2,1)S(1)} %get-tuple-element.34), kind=kOutput, calls=%fused_computation.12 | convolution fusion | flops 1625292800 | bytes 8126464 | tf_op jit(solution)/shard_map/dot_general | solution.py:27
  78.1 1.5 %collective-permute-start.3 = (bf16[256,2048]{1,0:T(8,128)(2,1)}, bf16[256,2048]{1,0:T(8,128)(2,1)}, u32[]{:S(2)}, u32[]{:S(2)}) collective-permute-start(bf16[256,2048]{1,0:T(8,128)(2,1)} %bitcast.10), channel_id=1, source_target_pairs={{0,16},{8,24},{16,0},{24,8},{1,17},{9,25},{17,1},{25,9},{2,18},{10... | collective-permute-start | bytes 3145736 | tf_op jit(solution)/shard_map/ppermute | solution.py:70
  79.6 0.0 collective-permute-start.1
  79.6 1.8 %fusion.84 = f32[256,384]{0,1:T(8,128)S(1)} fusion(bf16[256,2048]{1,0:T(8,128)(2,1)} %bitcast.5, bf16[192,2048]{1,0:T(8,128)(2,1)S(1)} %copy-done.4, bf16[192,2048]{1,0:T(8,128)(2,1)S(1)} %copy-done.6), kind=kOutput, calls=%fused_computation.118 | convolution fusion | flops 405798912 | bytes 3014656 | tf_op jit(solution)/shard_map/dot_general | solution.py:15
  81.4 1.7 %multiply_convert_fusion.15 = (bf16[256,192]{0,1:T(8,128)(2,1)S(1)}, bf16[256,192]{0,1:T(8,128)(2,1)S(1)}) fusion(f32[256,384]{0,1:T(8,128)S(1)} %fusion.84, bf16[256,2048]{1,0:T(8,128)(2,1)} %bitcast.10, bf16[1,768,2048]{2,1,0:T(8,128)(2,1)S(1)} %copy-done, s32[]{:T(128)S(6)} %select_n.28), kind=kOutput, calls=%fused_computation.86 | convolution fusion | flops 201965568 | bytes 2424836 | tf_op jit(solution)/shard_map/dot_general | solution.py:15
  83.2 2.8 %fusion.58 = f32[192,2048]{1,0:T(8,128)} fusion(bf16[256,2048]{1,0:T(8,128)(2,1)} %bitcast.10, f32[256,384]{0,1:T(8,128)S(1)} %fusion.84), kind=kOutput, calls=%fused_computation.93 | convolution fusion | flops 201621504 | bytes 3014656 | tf_op jit(solution)/shard_map/dot_general | solution.py:21
  85.9 3.4 %fusion.32 = f32[384,2048]{1,0:T(8,128)} fusion(bf16[256,2048]{1,0:T(8,128)(2,1)} %bitcast.5, bf16[256,192]{0,1:T(8,128)(2,1)S(1)} %get-tuple-element.43, bf16[256,192]{0,1:T(8,128)(2,1)S(1)} %get-tuple-element.42), kind=kOutput, calls=%fused_computation.53 | convolution fusion | flops 403046400 | bytes 4390912 | tf_op jit(solution)/shard_map/dot_general | solution.py:21
  89.4 7.6 %all-to-all-done.2 = bf16[8,32,2048]{2,1,0:T(8,128)(2,1)} async-done(((bf16[8,32,2048]{2,1,0:T(8,128)(2,1)}), bf16[8,32,2048]{2,1,0:T(8,128)(2,1)}, u32[]{:S(2)}, u32[]{:S(2)}) %all-to-all-start.2) | async-done | bytes 1048608 | tf_op jit(solution)/shard_map/all_to_all | solution.py:90
  97.0 4.4 %all-to-all-start.3 = ((bf16[8,32,2048]{2,1,0:T(8,128)(2,1)}), bf16[8,32,2048]{2,1,0:T(8,128)(2,1)}, u32[]{:S(2)}, u32[]{:S(2)}) async-start(bf16[8,32,2048]{2,1,0:T(8,128)(2,1)} %bitcast.76), calls=%async_computation.3 | async-start | bytes 2097152 | tf_op jit(solution)/shard_map/all_to_all | solution.py:107
  101.4 0.0 copy-start.5
  101.4 0.0 copy-start.7
  101.4 0.0 collective-permute-done
  101.5 0.0 collective-permute-done.1
  101.5 2.8 %broadcast_multiply_fusion = (bf16[256,2048]{1,0:T(8,128)(2,1)}, f32[256,2048]{1,0:T(8,128)S(1)}) fusion(f32[256]{0:T(256)S(1)} %bitcast.85, bf16[256,2048]{1,0:T(8,128)(2,1)} %bitcast.12, s32[256]{0:T(256)S(1)} %bitcast.82), kind=kOutput, calls=%fused_computation.23 | convolution fusion | flops 269549568 | bytes 4196352 | tf_op jit(solution)/shard_map/dot_general | solution.py:27
  104.3 0.0 collective-permute-done.2
  104.3 0.0 collective-permute-done.3
  104.3 1.8 %fusion.82 = f32[256,384]{0,1:T(8,128)S(1)} fusion(bf16[256,2048]{1,0:T(8,128)(2,1)} %collective-permute-done.2, bf16[192,2048]{1,0:T(8,128)(2,1)S(1)} %copy-done.5, bf16[192,2048]{1,0:T(8,128)(2,1)S(1)} %copy-done.7), kind=kOutput, calls=%fused_computation.116 | convolution fusion | flops 405798912 | bytes 3014656 | tf_op jit(solution)/shard_map/dot_general | solution.py:15
  106.1 0.1 collective-permute-start.5
  106.2 1.8 %fusion.83 = f32[256,384]{0,1:T(8,128)S(1)} fusion(bf16[256,2048]{1,0:T(8,128)(2,1)} %collective-permute-done, bf16[192,2048]{1,0:T(8,128)(2,1)S(1)} %copy-done.5, bf16[192,2048]{1,0:T(8,128)(2,1)S(1)} %copy-done.7), kind=kOutput, calls=%fused_computation.117 | convolution fusion | flops 405798912 | bytes 3014656 | tf_op jit(solution)/shard_map/dot_general | solution.py:15
  108.0 0.6 collective-permute-start.4
  108.6 1.7 %multiply_convert_fusion.11 = (bf16[256,192]{0,1:T(8,128)(2,1)S(1)}, bf16[256,192]{0,1:T(8,128)(2,1)S(1)}) fusion(f32[256,384]{0,1:T(8,128)S(1)} %fusion.82, bf16[256,2048]{1,0:T(8,128)(2,1)} %collective-permute-done.3, bf16[1,768,2048]{2,1,0:T(8,128)(2,1)S(1)} %copy-done, s32[]{:T(128)S(6)} %select_n.28), kind=kOutput, calls=%fused_computation.78 | convolution fusion | flops 201965568 | bytes 2424836 | tf_op jit(solution)/shard_map/dot_general | solution.py:15
  110.3 0.0 copy-start.3
  110.3 1.8 %multiply_convert_fusion.13 = (bf16[256,192]{0,1:T(8,128)(2,1)S(1)}, bf16[256,192]{0,1:T(8,128)(2,1)S(1)}) fusion(f32[256,384]{0,1:T(8,128)S(1)} %fusion.83, bf16[256,2048]{1,0:T(8,128)(2,1)} %collective-permute-done.1, bf16[1,768,2048]{2,1,0:T(8,128)(2,1)S(1)} %copy-done, s32[]{:T(128)S(6)} %select_n.28), kind=kOutput, calls=%fused_computation.82 | convolution fusion | flops 201965568 | bytes 2424836 | tf_op jit(solution)/shard_map/dot_general | solution.py:15
  112.2 1.8 %fusion.36 = f32[384,2048]{1,0:T(8,128)S(1)} fusion(bf16[256,2048]{1,0:T(8,128)(2,1)} %collective-permute-done, bf16[256,192]{0,1:T(8,128)(2,1)S(1)} %get-tuple-element.41, bf16[256,192]{0,1:T(8,128)(2,1)S(1)} %get-tuple-element.40), kind=kOutput, calls=%fused_computation.57 | convolution fusion | flops 403046400 | bytes 4390912 | tf_op jit(solution)/shard_map/dot_general | solution.py:21
  114.0 0.3 multiply_reduce_fusion
  114.3 0.7 maximum_maximum_fusion
  115.0 1.8 %fusion.40 = f32[384,2048]{1,0:T(8,128)S(1)} fusion(bf16[256,2048]{1,0:T(8,128)(2,1)} %collective-permute-done.2, bf16[256,192]{0,1:T(8,128)(2,1)S(1)} %get-tuple-element.45, bf16[256,192]{0,1:T(8,128)(2,1)S(1)} %get-tuple-element.44), kind=kOutput, calls=%fused_computation.61 | convolution fusion | flops 403046400 | bytes 4390912 | tf_op jit(solution)/shard_map/dot_general | solution.py:21
  116.8 1.6 %convolution_add_fusion.1 = f32[192,2048]{1,0:T(8,128)S(1)} fusion(f32[192,2048]{1,0:T(8,128)S(1)} %copy-done.2, bf16[256,2048]{1,0:T(8,128)(2,1)} %collective-permute-done.1, f32[256,384]{0,1:T(8,128)S(1)} %fusion.83), kind=kOutput, calls=%fused_computation.10 | convolution fusion | flops 202014720 | bytes 4587520 | tf_op jit(solution)/shard_map/dot_general | solution.py:21
  118.4 0.0 collective-permute-done.5
  118.4 0.6 fusion.81
  119.0 0.0 collective-permute-done.4
  119.1 0.5 multiply_convert_fusion.9
  119.6 0.4 fusion.59
  120.0 2.7 %fusion.13 = bf16[1,192,2048]{2,1,0:T(8,128)(2,1)} fusion(f32[192,2048]{1,0:T(8,128)S(1)} %fusion.59, f32[192,2048]{1,0:T(8,128)S(1)} %convolution_add_fusion.1, bf16[256,2048]{1,0:T(8,128)(2,1)} %collective-permute-done.3, f32[256,384]{0,1:T(8,128)S(1)} %fusion.82), kind=kOutput, calls=%fused_computation.18 | convolution fusion | flops 202801152 | bytes 5373952 | tf_op jit(solution)/shard_map/dot_general | solution.py:21
  122.7 0.6 add_convert_fusion
  123.3 1.2 slice_bitcast_fusion
  124.5 2.1 %all-to-all-done.3 = bf16[8,32,2048]{2,1,0:T(8,128)(2,1)} async-done(((bf16[8,32,2048]{2,1,0:T(8,128)(2,1)}), bf16[8,32,2048]{2,1,0:T(8,128)(2,1)}, u32[]{:S(2)}, u32[]{:S(2)}) %all-to-all-start.3) | async-done | bytes 1048608 | tf_op jit(solution)/shard_map/all_to_all | solution.py:107
  126.6 2.7 %convolution_convert_fusion = bf16[256,2048]{1,0:T(8,128)(2,1)} fusion(bf16[256,2048]{1,0:T(8,128)(2,1)} %bitcast.14, s32[256]{0:T(256)S(1)} %bitcast.83), kind=kOutput, calls=%fused_computation.13 | convolution fusion | flops 269025280 | bytes 2098176 | tf_op jit(solution)/shard_map/dot_general | solution.py:27
  (20 shorter events, 0.0 us)
Async XLA Ops:
  0.6 51.8 %copy-start = (bf16[1,768,2048]{2,1,0:T(8,128)(2,1)S(1)}, bf16[1,768,2048]{2,1,0:T(8,128)(2,1)}, u32[]{:S(2)}) copy-start(bf16[1,768,2048]{2,1,0:T(8,128)(2,1)} %param.12) | copy-start | bytes 9437188
  4.4 33.1 %all-to-all-start = ((bf16[8,32,2048]{2,1,0:T(8,128)(2,1)}), bf16[8,32,2048]{2,1,0:T(8,128)(2,1)}, u32[]{:S(2)}, u32[]{:S(2)}) async-start(bf16[8,32,2048]{2,1,0:T(8,128)(2,1)} %bitcast.75), calls=%async_computation | async-start | bytes 2097152 | tf_op jit(solution)/shard_map/all_to_all | solution.py:56
  37.5 29.9 %all-to-all-start.1 = ((bf16[8,32,2048]{2,1,0:T(8,128)(2,1)}), bf16[8,32,2048]{2,1,0:T(8,128)(2,1)}, u32[]{:S(2)}, u32[]{:S(2)}) async-start(bf16[8,32,2048]{2,1,0:T(8,128)(2,1)} %bitcast.74), calls=%async_computation.1 | async-start | bytes 2097152 | tf_op jit(solution)/shard_map/all_to_all | solution.py:56
  42.0 5.2 %copy-start.8 = (bf16[1,768,2048]{2,1,0:T(8,128)(2,1)S(1)}, bf16[1,768,2048]{2,1,0:T(8,128)(2,1)}, u32[]{:S(2)}) copy-start(bf16[1,768,2048]{2,1,0:T(8,128)(2,1)} %param.11) | copy-start | bytes 9437188
  45.7 58.6 %collective-permute-start.2 = (bf16[256,2048]{1,0:T(8,128)(2,1)}, bf16[256,2048]{1,0:T(8,128)(2,1)}, u32[]{:S(2)}, u32[]{:S(2)}) collective-permute-start(bf16[256,2048]{1,0:T(8,128)(2,1)} %bitcast.5), channel_id=1, source_target_pairs={{0,16},{8,24},{16,0},{24,8},{1,17},{9,25},{17,1},{25,9},{2,18},{10... | collective-permute-start | bytes 3145736 | tf_op jit(solution)/shard_map/ppermute | solution.py:70
  47.2 54.3 %collective-permute-start = (bf16[256,2048]{1,0:T(8,128)(2,1)}, bf16[256,2048]{1,0:T(8,128)(2,1)}, u32[]{:S(2)}, u32[]{:S(2)}) collective-permute-start(bf16[256,2048]{1,0:T(8,128)(2,1)} %bitcast.5), channel_id=1, source_target_pairs={{0,8},{8,0},{16,24},{24,16},{1,9},{9,1},{17,25},{25,17},{2,10},{10... | collective-permute-start | bytes 3145736 | tf_op jit(solution)/shard_map/ppermute | solution.py:70
  51.2 1.2 copy-start.11
  67.3 29.6 %all-to-all-start.2 = ((bf16[8,32,2048]{2,1,0:T(8,128)(2,1)}), bf16[8,32,2048]{2,1,0:T(8,128)(2,1)}, u32[]{:S(2)}, u32[]{:S(2)}) async-start(bf16[8,32,2048]{2,1,0:T(8,128)(2,1)} %bitcast.77), calls=%async_computation.2 | async-start | bytes 2097152 | tf_op jit(solution)/shard_map/all_to_all | solution.py:90
  71.6 3.1 %copy-start.9 = (bf16[1,768,2048]{2,1,0:T(8,128)(2,1)S(1)}, bf16[1,768,2048]{2,1,0:T(8,128)(2,1)}, u32[]{:S(2)}) copy-start(bf16[1,768,2048]{2,1,0:T(8,128)(2,1)} %param.11) | copy-start | bytes 9437188
  71.6 3.6 %copy-start.10 = (bf16[1,768,2048]{2,1,0:T(8,128)(2,1)S(1)}, bf16[1,768,2048]{2,1,0:T(8,128)(2,1)}, u32[]{:S(2)}) copy-start(bf16[1,768,2048]{2,1,0:T(8,128)(2,1)} %param.10) | copy-start | bytes 9437188
  75.2 4.3 %copy-start.4 = (bf16[192,2048]{1,0:T(8,128)(2,1)S(1)}, bf16[192,2048]{1,0:T(8,128)(2,1)}, u32[]{:S(2)}) copy-start(bf16[192,2048]{1,0:T(8,128)(2,1)} %get-tuple-element.48) | copy-start | bytes 2359300
  75.2 4.3 %copy-start.6 = (bf16[192,2048]{1,0:T(8,128)(2,1)S(1)}, bf16[192,2048]{1,0:T(8,128)(2,1)}, u32[]{:S(2)}) copy-start(bf16[192,2048]{1,0:T(8,128)(2,1)} %get-tuple-element.49) | copy-start | bytes 2359300
  78.1 26.2 %collective-permute-start.3 = (bf16[256,2048]{1,0:T(8,128)(2,1)}, bf16[256,2048]{1,0:T(8,128)(2,1)}, u32[]{:S(2)}, u32[]{:S(2)}) collective-permute-start(bf16[256,2048]{1,0:T(8,128)(2,1)} %bitcast.10), channel_id=1, source_target_pairs={{0,16},{8,24},{16,0},{24,8},{1,17},{9,25},{17,1},{25,9},{2,18},{10... | collective-permute-start | bytes 3145736 | tf_op jit(solution)/shard_map/ppermute | solution.py:70
  79.6 21.9 %collective-permute-start.1 = (bf16[256,2048]{1,0:T(8,128)(2,1)}, bf16[256,2048]{1,0:T(8,128)(2,1)}, u32[]{:S(2)}, u32[]{:S(2)}) collective-permute-start(bf16[256,2048]{1,0:T(8,128)(2,1)} %bitcast.10), channel_id=1, source_target_pairs={{0,8},{8,0},{16,24},{24,16},{1,9},{9,1},{17,25},{25,17},{2,10},{10... | collective-permute-start | bytes 3145736 | tf_op jit(solution)/shard_map/ppermute | solution.py:70
  97.0 29.6 %all-to-all-start.3 = ((bf16[8,32,2048]{2,1,0:T(8,128)(2,1)}), bf16[8,32,2048]{2,1,0:T(8,128)(2,1)}, u32[]{:S(2)}, u32[]{:S(2)}) async-start(bf16[8,32,2048]{2,1,0:T(8,128)(2,1)} %bitcast.76), calls=%async_computation.3 | async-start | bytes 2097152 | tf_op jit(solution)/shard_map/all_to_all | solution.py:107
  101.4 2.9 %copy-start.5 = (bf16[192,2048]{1,0:T(8,128)(2,1)S(1)}, bf16[192,2048]{1,0:T(8,128)(2,1)}, u32[]{:S(2)}) copy-start(bf16[192,2048]{1,0:T(8,128)(2,1)} %get-tuple-element.48) | copy-start | bytes 2359300
  101.4 2.8 %copy-start.7 = (bf16[192,2048]{1,0:T(8,128)(2,1)S(1)}, bf16[192,2048]{1,0:T(8,128)(2,1)}, u32[]{:S(2)}) copy-start(bf16[192,2048]{1,0:T(8,128)(2,1)} %get-tuple-element.49) | copy-start | bytes 2359300
  106.1 12.3 %collective-permute-start.5 = (bf16[256,2048]{1,0:T(8,128)(2,1)}, bf16[256,2048]{1,0:T(8,128)(2,1)S(1)}, u32[]{:S(2)}, u32[]{:S(2)}) collective-permute-start(bf16[256,2048]{1,0:T(8,128)(2,1)} %collective-permute-done.2), channel_id=1, source_target_pairs={{0,8},{8,0},{16,24},{24,16},{1,9},{9,1},{17,25},{25,17},{2,10},{10... | collective-permute-start | bytes 3145736 | tf_op jit(solution)/shard_map/ppermute | solution.py:70
  108.0 11.0 %collective-permute-start.4 = (bf16[256,2048]{1,0:T(8,128)(2,1)}, bf16[256,2048]{1,0:T(8,128)(2,1)S(1)}, u32[]{:S(2)}, u32[]{:S(2)}) collective-permute-start(bf16[256,2048]{1,0:T(8,128)(2,1)} %collective-permute-done.3), channel_id=1, source_target_pairs={{0,8},{8,0},{16,24},{24,16},{1,9},{9,1},{17,25},{25,17},{2,10},{10... | collective-permute-start | bytes 3145736 | tf_op jit(solution)/shard_map/ppermute | solution.py:70
  110.3 3.7 %copy-start.3 = (bf16[256,2048]{1,0:T(8,128)(2,1)S(1)}, bf16[256,2048]{1,0:T(8,128)(2,1)}, u32[]{:S(2)}) copy-start(bf16[256,2048]{1,0:T(8,128)(2,1)} %param.13) | copy-start | bytes 3145732
  114.0 2.8 %copy-start.2 = (f32[192,2048]{1,0:T(8,128)S(1)}, f32[192,2048]{1,0:T(8,128)}, u32[]{:S(2)}) copy-start(f32[192,2048]{1,0:T(8,128)} %fusion.58) | copy-start | bytes 4718596
  120.0 2.7 %copy-start.1 = (f32[384,2048]{1,0:T(8,128)S(1)}, f32[384,2048]{1,0:T(8,128)}, u32[]{:S(2)}) copy-start(f32[384,2048]{1,0:T(8,128)} %fusion.32) | copy-start | bytes 9437188
where the time goes:
time: 130 us; the launch traced here: 129 us
  matrix products  49.9 us (38%)
  waiting for transfers between devices  45.1 us (35%)
  starting transfers between devices  23.8 us (18%)
  local copies, waits for them, and re-layouts  7.6 us (6%)
  other arithmetic  1.94 us (1%)
    all_to_all x2, waiting for transfers between devices, exchange(): lax.all_to_all(rows.reshape(experts, per_pair, feature_width), 'ep', spli...  35.4 us
    dot_general x10, matrix products, rows_times(): lax.dot_general(left, right, (((1,), (1,)), ((), ())), preferred_element_...  19 us
    dot_general x7, matrix products, matmul(): return jnp.dot(left, right, preferred_element_type=jnp.float32)  15.8 us
    dot_general x8, matrix products, inner_rows(): lax.dot_general(left, right, (((0,), (0,)), ((), ())), preferred_element_...  15.1 us
    all_to_all x2, starting transfers between devices, exchange(): lax.all_to_all(rows.reshape(experts, per_pair, feature_width), 'ep', spli...  11.5 us
    all_to_all x1, waiting for transfers between devices, body(): lax.all_to_all(expert_out.reshape(experts, per_pair, feature_width), 'ep'...  7.62 us
    all_to_all x1, starting transfers between devices, body(): lax.all_to_all(token_part.reshape(experts, per_pair, feature_width), 'ep'...  4.41 us
    all_to_all x1, starting transfers between devices, body(): lax.all_to_all(expert_out.reshape(experts, per_pair, feature_width), 'ep'...  4.24 us
  transfers between devices with their start and end apart: 10, of which 4 were waited for; matrix products, arithmetic and copies ran while one was open for 40% of the time, Pallas kernels for 0%

commit v1 on v0

--- a/solution.py
+++ b/solution.py
@@ -4,6 +4,22 @@
 from jax.sharding import PartitionSpec as P
 
 STRIPE = 16
+
+
+def swapped_with_each(x, axis, split, join):
+    ways, here = (lax.axis_size(axis), lax.axis_index(axis))
+    width = x.shape[split] // ways
+    dims = list(x.shape)
+    dims[split] = width
+    height = dims[join]
+    dims[join] = height * ways
+    full = jnp.zeros(dims, x.dtype)
+    for mask in range(ways):
+        part = lax.dynamic_slice_in_dim(x, (here ^ mask) * width, width, axis=split)
+        if mask:
+            part = lax.ppermute(part, axis, [(d, d ^ mask) for d in range(ways)])
+        full = lax.dynamic_update_slice_in_dim(full, part, (here ^ mask) * height, axis=join)
+    return full
 
 
 def silu_grad(value):
@@ -104,12 +120,8 @@
         token_part, grad_out = lax.optimization_barrier((token_part, grad_in))
         far_grad = to_copy(grad_out, 2)
         near_grad = to_copy(grad_out, 1)
-    part_back = lax.all_to_all(
-        token_part.reshape(experts, per_pair, feature_width),
-        "ep",
-        split_axis=0,
-        concat_axis=0,
-        tiled=True,
+    part_back = swapped_with_each(
+        token_part.reshape(experts, per_pair, feature_width), "ep", 0, 0
     ).reshape(total_slots, feature_width)
     if by_pieces:
         returned, near_rows, near_grad = lax.optimization_barrier((returned, near_rows, near_grad))

time: 130 us -> 176 us (1.35)
  waiting for transfers between devices: 45.1 us -> 71.9 us
  starting transfers between devices: 23.8 us -> 33.9 us
  local copies, waits for them, and re-layouts: 7.6 us -> 16.2 us
    ppermute x0 -> x7, waiting for transfers between devices: none -> 36.5 us  [swapped_with_each(): part = lax.ppermute(part, axis, [(d, d ^ mask) for d in range(ways)])]
    ppermute x0 -> x7, starting transfers between devices: none -> 14.3 us  [swapped_with_each(): part = lax.ppermute(part, axis, [(d, d ^ mask) for d in range(ways)])]
    all_to_all x1, waiting for transfers between devices: 7.62 us -> 0.01 us  [body(): lax.all_to_all(expert_out.reshape(experts, per_pair, feature_width), 'ep'...]
    dynamic_update_slice x0 -> x7, local copies, waits for them, and re-layouts: none -> 4.59 us  [swapped_with_each(): lax.dynamic_update_slice_in_dim(full, part, (here ^ mask) * height, axis=...]
    all_to_all x1 -> x0, starting transfers between devices: 4.41 us -> none  [body(): lax.all_to_all(token_part.reshape(experts, per_pair, feature_width), 'ep'...]
    all_to_all x1 -> x0, waiting for transfers between devices: 2.11 us -> none  [body(): lax.all_to_all(token_part.reshape(experts, per_pair, feature_width), 'ep'...]
    dynamic_slice x0 -> x1, local copies, waits for them, and re-layouts: none -> 2.05 us  [swapped_with_each(): part = lax.dynamic_slice_in_dim(x, (here ^ mask) * width, width, axis=split)]
  transfers between devices with their start and end apart: 10 -> 16, of which waited for: 4 -> 8; matrix products, arithmetic and copies ran while one was open for 40% -> 30% of each run, Pallas kernels for 0% -> 0%
where the time goes in v1:
time: 176 us; the launch traced here: 175 us
  waiting for transfers between devices  71.9 us (41%)
  matrix products  49.7 us (28%)
  starting transfers between devices  33.9 us (19%)
  local copies, waits for them, and re-layouts  16.2 us (9%)
  other arithmetic  1.94 us (1%)
    ppermute x7, waiting for transfers between devices, swapped_with_each(): part = lax.ppermute(part, axis, [(d, d ^ mask) for d in range(ways)])  36.5 us
    all_to_all x2, waiting for transfers between devices, exchange(): lax.all_to_all(rows.reshape(experts, per_pair, feature_width), 'ep', spli...  35.3 us
    dot_general x10, matrix products, rows_times(): lax.dot_general(left, right, (((1,), (1,)), ((), ())), preferred_element_...  19 us
    dot_general x7, matrix products, matmul(): return jnp.dot(left, right, preferred_element_type=jnp.float32)  15.7 us
    dot_general x8, matrix products, inner_rows(): lax.dot_general(left, right, (((0,), (0,)), ((), ())), preferred_element_...  15 us
    ppermute x7, starting transfers between devices, swapped_with_each(): part = lax.ppermute(part, axis, [(d, d ^ mask) for d in range(ways)])  14.3 us
    all_to_all x2, starting transfers between devices, exchange(): lax.all_to_all(rows.reshape(experts, per_pair, feature_width), 'ep', spli...  11.5 us
    dynamic_update_slice x7, local copies, waits for them, and re-layouts, swapped_with_each(): lax.dynamic_update_slice_in_dim(full, part, (here ^ mask) * height, axis=...  4.59 us
  transfers between devices with their start and end apart: 16, of which 8 were waited for; matrix products, arithmetic and copies ran while one was open for 30% of the time, Pallas kernels for 0%

profile of v1, /device:TPU:0, one launch (start us, length us, event | category | flops | bytes accessed | tf_op | source)
XLA Modules:
  0.0 174.6 jit_solution(5577957261565460617)
XLA Ops:
  0.6 0.9 slice.45
  1.7 2.6 %convolution_convert_fusion.1 = bf16[256,2048]{1,0:T(8,128)(2,1)} fusion(bf16[256,2048]{1,0:T(8,128)(2,1)} %param.7, s32[256]{0:T(256)S(1)} %compare_select_fusion.1), kind=kOutput, calls=%fused_computation.14 | convolution fusion | flops 269025280 | bytes 2098176 | tf_op jit(solution)/shard_map/dot_general | solution.py:43
  4.4 7.3 %all-to-all-start = ((bf16[8,32,2048]{2,1,0:T(8,128)(2,1)}), bf16[8,32,2048]{2,1,0:T(8,128)(2,1)}, u32[]{:S(2)}, u32[]{:S(2)}) async-start(bf16[8,32,2048]{2,1,0:T(8,128)(2,1)} %bitcast.75), calls=%async_computation | async-start | bytes 2097152 | tf_op jit(solution)/shard_map/all_to_all | solution.py:72
  11.6 0.7 slice.44
  12.4 2.6 %fusion.6 = bf16[256,2048]{1,0:T(8,128)(2,1)} fusion(bf16[256,2048]{1,0:T(8,128)(2,1)} %param.13, f32[256]{0:T(256)S(1)} %select_reduce_fusion, s32[256]{0:T(256)S(1)} %compare_select_fusion.1), kind=kOutput, calls=%fused_computation.11 | convolution fusion | flops 269549568 | bytes 2099200 | tf_op jit(solution)/shard_map/dot_general | solution.py:43
  15.1 22.4 %all-to-all-done = bf16[8,32,2048]{2,1,0:T(8,128)(2,1)} async-done(((bf16[8,32,2048]{2,1,0:T(8,128)(2,1)}), bf16[8,32,2048]{2,1,0:T(8,128)(2,1)}, u32[]{:S(2)}, u32[]{:S(2)}) %all-to-all-start) | async-done | bytes 1048608 | tf_op jit(solution)/shard_map/all_to_all | solution.py:72
  37.5 4.2 %all-to-all-start.1 = ((bf16[8,32,2048]{2,1,0:T(8,128)(2,1)}), bf16[8,32,2048]{2,1,0:T(8,128)(2,1)}, u32[]{:S(2)}, u32[]{:S(2)}) async-start(bf16[8,32,2048]{2,1,0:T(8,128)(2,1)} %bitcast.74), calls=%async_computation.1 | async-start | bytes 2097152 | tf_op jit(solution)/shard_map/all_to_all | solution.py:72
  42.0 0.9 compare_select_fusion
  42.9 2.8 %dynamic-slice_bitcast_fusion = (bf16[192,2048]{1,0:T(8,128)(2,1)}, bf16[192,2048]{1,0:T(8,128)(2,1)}) fusion(bf16[1,768,2048]{2,1,0:T(8,128)(2,1)} %param.11, s32[]{:T(128)S(6)} %select_n.68, bf16[1,768,2048]{2,1,0:T(8,128)(2,1)} %param.10), kind=kLoop, calls=%fused_computation.37 | loop fusion | bytes 3145732 | tf_op jit(solution)/shard_map/dynamic_slice | solution.py:155
  45.7 1.5 collective-permute-start.2
  47.2 4.0 %fusion.1 = f32[256,1536]{1,0:T(8,128)S(1)} fusion(bf16[256,2048]{1,0:T(8,128)(2,1)} %bitcast.5, bf16[768,2048]{1,0:T(8,128)(2,1)S(1)} %bitcast.78, bf16[768,2048]{1,0:T(8,128)(2,1)} %bitcast.80), kind=kOutput, calls=%fused_computation.2 | convolution fusion | flops 1623195648 | bytes 8912896 | tf_op jit(solution)/shard_map/dot_general | solution.py:31
  51.2 1.2 copy-done.11
  52.4 2.0 %fusion.9 = bf16[256,2048]{1,0:T(8,128)(2,1)} fusion(bf16[1,768,2048]{2,1,0:T(8,128)(2,1)S(1)} %copy-done, f32[256,1536]{1,0:T(8,128)S(1)} %fusion.1), kind=kOutput, calls=%fused_computation.16 | convolution fusion | flops 807010304 | bytes 5767168 | tf_op jit(solution)/shard_map/dot_general | solution.py:43
  54.5 12.9 %all-to-all-done.1 = bf16[8,32,2048]{2,1,0:T(8,128)(2,1)} async-done(((bf16[8,32,2048]{2,1,0:T(8,128)(2,1)}), bf16[8,32,2048]{2,1,0:T(8,128)(2,1)}, u32[]{:S(2)}, u32[]{:S(2)}) %all-to-all-start.1) | async-done | bytes 1048608 | tf_op jit(solution)/shard_map/all_to_all | solution.py:72
  67.3 3.0 %multiply_convert_fusion.1 = (bf16[256,768]{1,0:T(8,128)(2,1)S(1)}, bf16[256,768]{1,0:T(8,128)(2,1)S(1)}) fusion(f32[256,1536]{1,0:T(8,128)} %copy-done.11, bf16[256,2048]{1,0:T(8,128)(2,1)} %bitcast.10, bf16[1,768,2048]{2,1,0:T(8,128)(2,1)S(1)} %copy-done), kind=kOutput, calls=%fused_computation.40 | convolution fusion | flops 807862272 | bytes 6553600 | tf_op jit(solution)/shard_map/dot_general | solution.py:31
  70.4 0.6 copy-done.10
  71.0 2.8 %fusion.7 = bf16[256,2048]{1,0:T(8,128)(2,1)} fusion(bf16[768,2048]{1,0:T(8,128)(2,1)S(1)} %bitcast.79, bf16[768,2048]{1,0:T(8,128)(2,1)S(1)} %bitcast.81, bf16[256,768]{1,0:T(8,128)(2,1)S(1)} %get-tuple-element.35, bf16[256,768]{1,0:T(8,128)(2,1)S(1)} %get-tuple-element.34), kind=kOutput, calls=%fused_computation.12 | convolution fusion | flops 1625292800 | bytes 8126464 | tf_op jit(solution)/shard_map/dot_general | solution.py:43
  73.7 1.5 collective-permute-start.3
  75.3 4.4 %all-to-all-start.2 = ((bf16[8,32,2048]{2,1,0:T(8,128)(2,1)}), bf16[8,32,2048]{2,1,0:T(8,128)(2,1)}, u32[]{:S(2)}, u32[]{:S(2)}) async-start(bf16[8,32,2048]{2,1,0:T(8,128)(2,1)} %bitcast.76), calls=%async_computation.2 | async-start | bytes 2097152 | tf_op jit(solution)/shard_map/all_to_all | solution.py:106
  79.7 1.2 broadcast_in_dim.46
  80.9 2.0 %constant_dynamic-slice_fusion = (bf16[1,32,2048]{2,1,0:T(8,128)(2,1)S(1)}, bf16[1,32,2048]{2,1,0:T(8,128)(2,1)S(1)}, bf16[1,32,2048]{2,1,0:T(8,128)(2,1)S(1)}, ...) fusion(bf16[8,32,2048]{2,1,0:T(8,128)(2,1)} %bitcast.77, ...), kind=kLoop, calls=%fused_computation.102 | loop fusion | bytes 2097184 | tf_op jit(solution)/shard_map/dynamic_slice | solution.py:18
  82.9 1.7 collective-permute-start.4
  84.6 1.8 %fusion.84 = f32[256,384]{0,1:T(8,128)S(1)} fusion(bf16[256,2048]{1,0:T(8,128)(2,1)} %bitcast.5, bf16[192,2048]{1,0:T(8,128)(2,1)S(1)} %copy-done.4, bf16[192,2048]{1,0:T(8,128)(2,1)S(1)} %copy-done.6), kind=kOutput, calls=%fused_computation.133 | convolution fusion | flops 405798912 | bytes 3014656 | tf_op jit(solution)/shard_map/dot_general | solution.py:31
  86.5 1.7 multiply_convert_fusion.15
  88.2 3.4 %fusion.32 = f32[384,2048]{1,0:T(8,128)} fusion(bf16[256,2048]{1,0:T(8,128)(2,1)} %bitcast.5, bf16[256,192]{0,1:T(8,128)(2,1)S(1)} %get-tuple-element.51, bf16[256,192]{0,1:T(8,128)(2,1)S(1)} %get-tuple-element.50), kind=kOutput, calls=%fused_computation.53 | convolution fusion | flops 403046400 | bytes 4390912 | tf_op jit(solution)/shard_map/dot_general | solution.py:37
  91.6 2.8 %fusion.58 = f32[192,2048]{1,0:T(8,128)} fusion(bf16[256,2048]{1,0:T(8,128)(2,1)} %bitcast.10, f32[256,384]{0,1:T(8,128)S(1)} %fusion.84), kind=kOutput, calls=%fused_computation.94 | convolution fusion | flops 201621504 | bytes 3014656 | tf_op jit(solution)/shard_map/dot_general | solution.py:37
  94.4 1.5 collective-permute-start.5
  95.9 0.6 constant_dynamic-update-slice_fusion.6
  96.6 4.9 %collective-permute-done.5 = bf16[1,32,2048]{2,1,0:T(8,128)(2,1)S(1)} collective-permute-done((bf16[1,32,2048]{2,1,0:T(8,128)(2,1)S(1)}, bf16[1,32,2048]{2,1,0:T(8,128)(2,1)S(1)}, u32[]{:S(2)}, u32[]{:S(2)}) %collective-permute-start.5) | collective-permute-done | bytes 131104 | tf_op jit(solution)/shard_map/ppermute | solution.py:20
  101.5 3.0 %collective-permute-start.6 = (bf16[1,32,2048]{2,1,0:T(8,128)(2,1)S(1)}, bf16[1,32,2048]{2,1,0:T(8,128)(2,1)S(1)}, u32[]{:S(2)}, u32[]{:S(2)}) collective-permute-start(bf16[1,32,2048]{2,1,0:T(8,128)(2,1)S(1)} %get-tuple-element.42), channel_id=1, source_target_pairs={{0,3},{1,2},{2,1},{3,0},{4,7},{5,6},{6,5},{7,4},{8,11},{9,10},{10,... | collective-permute-start | bytes 393224 | tf_op jit(solution)/shard_map/ppermute | solution.py:20
  104.5 0.6 constant_dynamic-update-slice_fusion.5
  105.1 4.7 %collective-permute-done.6 = bf16[1,32,2048]{2,1,0:T(8,128)(2,1)S(1)} collective-permute-done((bf16[1,32,2048]{2,1,0:T(8,128)(2,1)S(1)}, bf16[1,32,2048]{2,1,0:T(8,128)(2,1)S(1)}, u32[]{:S(2)}, u32[]{:S(2)}) %collective-permute-start.6) | collective-permute-done | bytes 131104 | tf_op jit(solution)/shard_map/ppermute | solution.py:20
  109.9 6.3 %collective-permute-start.7 = (bf16[1,32,2048]{2,1,0:T(8,128)(2,1)S(1)}, bf16[1,32,2048]{2,1,0:T(8,128)(2,1)S(1)}, u32[]{:S(2)}, u32[]{:S(2)}) collective-permute-start(bf16[1,32,2048]{2,1,0:T(8,128)(2,1)S(1)} %get-tuple-element.41), channel_id=1, source_target_pairs={{0,4},{1,5},{2,6},{3,7},{4,0},{5,1},{6,2},{7,3},{8,12},{9,13},{10,... | collective-permute-start | bytes 393224 | tf_op jit(solution)/shard_map/ppermute | solution.py:20
  116.2 0.7 constant_dynamic-update-slice_fusion.4
  116.8 5.5 %collective-permute-done.7 = bf16[1,32,2048]{2,1,0:T(8,128)(2,1)S(1)} collective-permute-done((bf16[1,32,2048]{2,1,0:T(8,128)(2,1)S(1)}, bf16[1,32,2048]{2,1,0:T(8,128)(2,1)S(1)}, u32[]{:S(2)}, u32[]{:S(2)}) %collective-permute-start.7) | collective-permute-done | bytes 131104 | tf_op jit(solution)/shard_map/ppermute | solution.py:20
  122.3 0.3 collective-permute-start.8
  122.6 0.7 constant_dynamic-update-slice_fusion.3
  123.2 9.9 %collective-permute-done.8 = bf16[1,32,2048]{2,1,0:T(8,128)(2,1)S(1)} collective-permute-done((bf16[1,32,2048]{2,1,0:T(8,128)(2,1)S(1)}, bf16[1,32,2048]{2,1,0:T(8,128)(2,1)S(1)}, u32[]{:S(2)}, u32[]{:S(2)}) %collective-permute-start.8) | collective-permute-done | bytes 131104 | tf_op jit(solution)/shard_map/ppermute | solution.py:20
  133.1 0.4 collective-permute-start.9
  133.5 0.7 constant_dynamic-update-slice_fusion.2
  134.2 5.7 %collective-permute-done.9 = bf16[1,32,2048]{2,1,0:T(8,128)(2,1)S(1)} collective-permute-done((bf16[1,32,2048]{2,1,0:T(8,128)(2,1)S(1)}, bf16[1,32,2048]{2,1,0:T(8,128)(2,1)S(1)}, u32[]{:S(2)}, u32[]{:S(2)}) %collective-permute-start.9) | collective-permute-done | bytes 131104 | tf_op jit(solution)/shard_map/ppermute | solution.py:20
  139.9 1.1 collective-permute-start.10
  141.0 0.7 constant_dynamic-update-slice_fusion.1
  141.7 5.9 %collective-permute-done.10 = bf16[1,32,2048]{2,1,0:T(8,128)(2,1)S(1)} collective-permute-done((bf16[1,32,2048]{2,1,0:T(8,128)(2,1)S(1)}, bf16[1,32,2048]{2,1,0:T(8,128)(2,1)S(1)}, u32[]{:S(2)}, u32[]{:S(2)}) %collective-permute-start.10) | collective-permute-done | bytes 131104 | tf_op jit(solution)/shard_map/ppermute | solution.py:20
  147.5 0.7 constant_dynamic-update-slice_fusion
  148.2 2.8 %broadcast_multiply_fusion = (bf16[256,2048]{1,0:T(8,128)(2,1)}, f32[256,2048]{1,0:T(8,128)S(1)}) fusion(f32[256]{0:T(256)S(1)} %bitcast.85, bf16[256,2048]{1,0:T(8,128)(2,1)} %bitcast.12, s32[256]{0:T(256)S(1)} %bitcast.82), kind=kOutput, calls=%fused_computation.23 | convolution fusion | flops 269549568 | bytes 4196352 | tf_op jit(solution)/shard_map/dot_general | solution.py:43
  151.1 1.8 %fusion.82 = f32[256,384]{0,1:T(8,128)S(1)} fusion(bf16[256,2048]{1,0:T(8,128)(2,1)} %collective-permute-done.2, bf16[192,2048]{1,0:T(8,128)(2,1)S(1)} %copy-done.5, bf16[192,2048]{1,0:T(8,128)(2,1)S(1)} %copy-done.7), kind=kOutput, calls=%fused_computation.131 | convolution fusion | flops 405798912 | bytes 3014656 | tf_op jit(solution)/shard_map/dot_general | solution.py:31
  153.0 1.8 %fusion.83 = f32[256,384]{0,1:T(8,128)S(1)} fusion(bf16[256,2048]{1,0:T(8,128)(2,1)} %collective-permute-done, bf16[192,2048]{1,0:T(8,128)(2,1)S(1)} %copy-done.5, bf16[192,2048]{1,0:T(8,128)(2,1)S(1)} %copy-done.7), kind=kOutput, calls=%fused_computation.132 | convolution fusion | flops 405798912 | bytes 3014656 | tf_op jit(solution)/shard_map/dot_general | solution.py:31
  154.8 0.6 collective-permute-start.11
  155.4 1.7 multiply_convert_fusion.11
  157.1 1.8 %multiply_convert_fusion.13 = (bf16[256,192]{0,1:T(8,128)(2,1)S(1)}, bf16[256,192]{0,1:T(8,128)(2,1)S(1)}) fusion(f32[256,384]{0,1:T(8,128)S(1)} %fusion.83, bf16[256,2048]{1,0:T(8,128)(2,1)} %collective-permute-done.1, bf16[1,768,2048]{2,1,0:T(8,128)(2,1)S(1)} %copy-done, s32[]{:T(128)S(6)} %select_n.68), kind=kOutput, calls=%fused_computation.82 | convolution fusion | flops 201965568 | bytes 2424836 | tf_op jit(solution)/shard_map/dot_general | solution.py:31
  158.9 1.8 %fusion.36 = f32[384,2048]{1,0:T(8,128)S(1)} fusion(bf16[256,2048]{1,0:T(8,128)(2,1)} %collective-permute-done, bf16[256,192]{0,1:T(8,128)(2,1)S(1)} %get-tuple-element.49, bf16[256,192]{0,1:T(8,128)(2,1)S(1)} %get-tuple-element.48), kind=kOutput, calls=%fused_computation.57 | convolution fusion | flops 403046400 | bytes 4390912 | tf_op jit(solution)/shard_map/dot_general | solution.py:37
  160.8 0.3 multiply_reduce_fusion
  161.1 0.7 maximum_maximum_fusion
  161.7 1.8 %fusion.40 = f32[384,2048]{1,0:T(8,128)S(1)} fusion(bf16[256,2048]{1,0:T(8,128)(2,1)} %collective-permute-done.2, bf16[256,192]{0,1:T(8,128)(2,1)S(1)} %get-tuple-element.53, bf16[256,192]{0,1:T(8,128)(2,1)S(1)} %get-tuple-element.52), kind=kOutput, calls=%fused_computation.61 | convolution fusion | flops 403046400 | bytes 4390912 | tf_op jit(solution)/shard_map/dot_general | solution.py:37
  163.6 1.6 convolution_add_fusion.1
  165.2 0.6 fusion.81
  165.8 0.5 multiply_convert_fusion.9
  166.3 0.7 copy-done.1
  167.1 0.6 add_convert_fusion
  167.7 1.2 slice_bitcast_fusion
  168.9 0.4 fusion.59
  169.3 2.6 %fusion.13 = bf16[1,192,2048]{2,1,0:T(8,128)(2,1)} fusion(f32[192,2048]{1,0:T(8,128)S(1)} %fusion.59, f32[192,2048]{1,0:T(8,128)S(1)} %convolution_add_fusion.1, bf16[256,2048]{1,0:T(8,128)(2,1)} %collective-permute-done.3, f32[256,384]{0,1:T(8,128)S(1)} %fusion.82), kind=kOutput, calls=%fused_computation.18 | convolution fusion | flops 202801152 | bytes 5373952 | tf_op jit(solution)/shard_map/dot_general | solution.py:37
  171.9 2.7 %convolution_convert_fusion = bf16[256,2048]{1,0:T(8,128)(2,1)} fusion(bf16[256,2048]{1,0:T(8,128)(2,1)} %bitcast.14, s32[256]{0:T(256)S(1)} %bitcast.83), kind=kOutput, calls=%fused_computation.13 | convolution fusion | flops 269025280 | bytes 2098176 | tf_op jit(solution)/shard_map/dot_general | solution.py:43
  (41 shorter events, 0.7 us)
Async XLA Ops:
  0.6 51.8 %copy-start = (bf16[1,768,2048]{2,1,0:T(8,128)(2,1)S(1)}, bf16[1,768,2048]{2,1,0:T(8,128)(2,1)}, u32[]{:S(2)}) copy-start(bf16[1,768,2048]{2,1,0:T(8,128)(2,1)} %param.12) | copy-start | bytes 9437188
  4.4 33.1 %all-to-all-start = ((bf16[8,32,2048]{2,1,0:T(8,128)(2,1)}), bf16[8,32,2048]{2,1,0:T(8,128)(2,1)}, u32[]{:S(2)}, u32[]{:S(2)}) async-start(bf16[8,32,2048]{2,1,0:T(8,128)(2,1)} %bitcast.75), calls=%async_computation | async-start | bytes 2097152 | tf_op jit(solution)/shard_map/all_to_all | solution.py:72
  37.5 29.9 %all-to-all-start.1 = ((bf16[8,32,2048]{2,1,0:T(8,128)(2,1)}), bf16[8,32,2048]{2,1,0:T(8,128)(2,1)}, u32[]{:S(2)}, u32[]{:S(2)}) async-start(bf16[8,32,2048]{2,1,0:T(8,128)(2,1)} %bitcast.74), calls=%async_computation.1 | async-start | bytes 2097152 | tf_op jit(solution)/shard_map/all_to_all | solution.py:72
  42.0 5.2 %copy-start.8 = (bf16[1,768,2048]{2,1,0:T(8,128)(2,1)S(1)}, bf16[1,768,2048]{2,1,0:T(8,128)(2,1)}, u32[]{:S(2)}) copy-start(bf16[1,768,2048]{2,1,0:T(8,128)(2,1)} %param.11) | copy-start | bytes 9437188
  45.7 105.4 %collective-permute-start.2 = (bf16[256,2048]{1,0:T(8,128)(2,1)}, bf16[256,2048]{1,0:T(8,128)(2,1)}, u32[]{:S(2)}, u32[]{:S(2)}) collective-permute-start(bf16[256,2048]{1,0:T(8,128)(2,1)} %bitcast.5), channel_id=1, source_target_pairs={{0,16},{8,24},{16,0},{24,8},{1,17},{9,25},{17,1},{25,9},{2,18},{10... | collective-permute-start | bytes 3145736 | tf_op jit(solution)/shard_map/ppermute | solution.py:86
  47.2 101.0 %collective-permute-start = (bf16[256,2048]{1,0:T(8,128)(2,1)}, bf16[256,2048]{1,0:T(8,128)(2,1)}, u32[]{:S(2)}, u32[]{:S(2)}) collective-permute-start(bf16[256,2048]{1,0:T(8,128)(2,1)} %bitcast.5), channel_id=1, source_target_pairs={{0,8},{8,0},{16,24},{24,16},{1,9},{9,1},{17,25},{25,17},{2,10},{10... | collective-permute-start | bytes 3145736 | tf_op jit(solution)/shard_map/ppermute | solution.py:86
  51.2 1.2 copy-start.11
  67.3 3.0 %copy-start.9 = (bf16[1,768,2048]{2,1,0:T(8,128)(2,1)S(1)}, bf16[1,768,2048]{2,1,0:T(8,128)(2,1)}, u32[]{:S(2)}) copy-start(bf16[1,768,2048]{2,1,0:T(8,128)(2,1)} %param.11) | copy-start | bytes 9437188
  67.3 3.6 %copy-start.10 = (bf16[1,768,2048]{2,1,0:T(8,128)(2,1)S(1)}, bf16[1,768,2048]{2,1,0:T(8,128)(2,1)}, u32[]{:S(2)}) copy-start(bf16[1,768,2048]{2,1,0:T(8,128)(2,1)} %param.10) | copy-start | bytes 9437188
  73.7 77.3 %collective-permute-start.3 = (bf16[256,2048]{1,0:T(8,128)(2,1)}, bf16[256,2048]{1,0:T(8,128)(2,1)}, u32[]{:S(2)}, u32[]{:S(2)}) collective-permute-start(bf16[256,2048]{1,0:T(8,128)(2,1)} %bitcast.10), channel_id=1, source_target_pairs={{0,16},{8,24},{16,0},{24,8},{1,17},{9,25},{17,1},{25,9},{2,18},{10... | collective-permute-start | bytes 3145736 | tf_op jit(solution)/shard_map/ppermute | solution.py:86
  75.3 72.9 %collective-permute-start.1 = (bf16[256,2048]{1,0:T(8,128)(2,1)}, bf16[256,2048]{1,0:T(8,128)(2,1)}, u32[]{:S(2)}, u32[]{:S(2)}) collective-permute-start(bf16[256,2048]{1,0:T(8,128)(2,1)} %bitcast.10), channel_id=1, source_target_pairs={{0,8},{8,0},{16,24},{24,16},{1,9},{9,1},{17,25},{25,17},{2,10},{10... | collective-permute-start | bytes 3145736 | tf_op jit(solution)/shard_map/ppermute | solution.py:86
  75.3 72.9 %all-to-all-start.2 = ((bf16[8,32,2048]{2,1,0:T(8,128)(2,1)}), bf16[8,32,2048]{2,1,0:T(8,128)(2,1)}, u32[]{:S(2)}, u32[]{:S(2)}) async-start(bf16[8,32,2048]{2,1,0:T(8,128)(2,1)} %bitcast.76), calls=%async_computation.2 | async-start | bytes 2097152 | tf_op jit(solution)/shard_map/all_to_all | solution.py:106
  79.7 4.9 %copy-start.4 = (bf16[192,2048]{1,0:T(8,128)(2,1)S(1)}, bf16[192,2048]{1,0:T(8,128)(2,1)}, u32[]{:S(2)}) copy-start(bf16[192,2048]{1,0:T(8,128)(2,1)} %get-tuple-element.56) | copy-start | bytes 2359300
  79.7 4.9 %copy-start.6 = (bf16[192,2048]{1,0:T(8,128)(2,1)S(1)}, bf16[192,2048]{1,0:T(8,128)(2,1)}, u32[]{:S(2)}) copy-start(bf16[192,2048]{1,0:T(8,128)(2,1)} %get-tuple-element.57) | copy-start | bytes 2359300
  82.9 11.5 %collective-permute-start.4 = (bf16[1,32,2048]{2,1,0:T(8,128)(2,1)S(1)}, bf16[1,32,2048]{2,1,0:T(8,128)(2,1)S(1)}, u32[]{:S(2)}, u32[]{:S(2)}) collective-permute-start(bf16[1,32,2048]{2,1,0:T(8,128)(2,1)S(1)} %get-tuple-element.44), channel_id=1, source_target_pairs={{0,1},{1,0},{2,3},{3,2},{4,5},{5,4},{6,7},{7,6},{8,9},{9,8},{10,11... | collective-permute-start | bytes 393224 | tf_op jit(solution)/shard_map/ppermute | solution.py:20
  94.4 7.0 %collective-permute-start.5 = (bf16[1,32,2048]{2,1,0:T(8,128)(2,1)S(1)}, bf16[1,32,2048]{2,1,0:T(8,128)(2,1)S(1)}, u32[]{:S(2)}, u32[]{:S(2)}) collective-permute-start(bf16[1,32,2048]{2,1,0:T(8,128)(2,1)S(1)} %get-tuple-element.43), channel_id=1, source_target_pairs={{0,2},{1,3},{2,0},{3,1},{4,6},{5,7},{6,4},{7,5},{8,10},{9,11},{10,... | collective-permute-start | bytes 393224 | tf_op jit(solution)/shard_map/ppermute | solution.py:20
  101.5 8.4 %collective-permute-start.6 = (bf16[1,32,2048]{2,1,0:T(8,128)(2,1)S(1)}, bf16[1,32,2048]{2,1,0:T(8,128)(2,1)S(1)}, u32[]{:S(2)}, u32[]{:S(2)}) collective-permute-start(bf16[1,32,2048]{2,1,0:T(8,128)(2,1)S(1)} %get-tuple-element.42), channel_id=1, source_target_pairs={{0,3},{1,2},{2,1},{3,0},{4,7},{5,6},{6,5},{7,4},{8,11},{9,10},{10,... | collective-permute-start | bytes 393224 | tf_op jit(solution)/shard_map/ppermute | solution.py:20
  109.9 12.4 %collective-permute-start.7 = (bf16[1,32,2048]{2,1,0:T(8,128)(2,1)S(1)}, bf16[1,32,2048]{2,1,0:T(8,128)(2,1)S(1)}, u32[]{:S(2)}, u32[]{:S(2)}) collective-permute-start(bf16[1,32,2048]{2,1,0:T(8,128)(2,1)S(1)} %get-tuple-element.41), channel_id=1, source_target_pairs={{0,4},{1,5},{2,6},{3,7},{4,0},{5,1},{6,2},{7,3},{8,12},{9,13},{10,... | collective-permute-start | bytes 393224 | tf_op jit(solution)/shard_map/ppermute | solution.py:20
  122.3 10.8 %collective-permute-start.8 = (bf16[1,32,2048]{2,1,0:T(8,128)(2,1)S(1)}, bf16[1,32,2048]{2,1,0:T(8,128)(2,1)S(1)}, u32[]{:S(2)}, u32[]{:S(2)}) collective-permute-start(bf16[1,32,2048]{2,1,0:T(8,128)(2,1)S(1)} %get-tuple-element.40), channel_id=1, source_target_pairs={{0,5},{1,4},{2,7},{3,6},{4,1},{5,0},{6,3},{7,2},{8,13},{9,12},{10,... | collective-permute-start | bytes 393224 | tf_op jit(solution)/shard_map/ppermute | solution.py:20
  133.1 6.8 %collective-permute-start.9 = (bf16[1,32,2048]{2,1,0:T(8,128)(2,1)S(1)}, bf16[1,32,2048]{2,1,0:T(8,128)(2,1)S(1)}, u32[]{:S(2)}, u32[]{:S(2)}) collective-permute-start(bf16[1,32,2048]{2,1,0:T(8,128)(2,1)S(1)} %get-tuple-element.39), channel_id=1, source_target_pairs={{0,6},{1,7},{2,4},{3,5},{4,2},{5,3},{6,0},{7,1},{8,14},{9,15},{10,... | collective-permute-start | bytes 393224 | tf_op jit(solution)/shard_map/ppermute | solution.py:20
  139.9 7.7 %collective-permute-start.10 = (bf16[1,32,2048]{2,1,0:T(8,128)(2,1)S(1)}, bf16[1,32,2048]{2,1,0:T(8,128)(2,1)S(1)}, u32[]{:S(2)}, u32[]{:S(2)}) collective-permute-start(bf16[1,32,2048]{2,1,0:T(8,128)(2,1)S(1)} %get-tuple-element.38), channel_id=1, source_target_pairs={{0,7},{1,6},{2,5},{3,4},{4,3},{5,2},{6,1},{7,0},{8,15},{9,14},{10,... | collective-permute-start | bytes 393224 | tf_op jit(solution)/shard_map/ppermute | solution.py:20
  148.2 2.8 %copy-start.5 = (bf16[192,2048]{1,0:T(8,128)(2,1)S(1)}, bf16[192,2048]{1,0:T(8,128)(2,1)}, u32[]{:S(2)}) copy-start(bf16[192,2048]{1,0:T(8,128)(2,1)} %get-tuple-element.56) | copy-start | bytes 2359300
  148.2 2.8 %copy-start.7 = (bf16[192,2048]{1,0:T(8,128)(2,1)S(1)}, bf16[192,2048]{1,0:T(8,128)(2,1)}, u32[]{:S(2)}) copy-start(bf16[192,2048]{1,0:T(8,128)(2,1)} %get-tuple-element.57) | copy-start | bytes 2359300
  152.9 12.3 %collective-permute-start.12 = (bf16[256,2048]{1,0:T(8,128)(2,1)}, bf16[256,2048]{1,0:T(8,128)(2,1)S(1)}, u32[]{:S(2)}, u32[]{:S(2)}) collective-permute-start(bf16[256,2048]{1,0:T(8,128)(2,1)} %collective-permute-done.2), channel_id=1, source_target_pairs={{0,8},{8,0},{16,24},{24,16},{1,9},{9,1},{17,25},{25,17},{2,10},{10... | collective-permute-start | bytes 3145736 | tf_op jit(solution)/shard_map/ppermute | solution.py:86
  154.8 11.0 %collective-permute-start.11 = (bf16[256,2048]{1,0:T(8,128)(2,1)}, bf16[256,2048]{1,0:T(8,128)(2,1)S(1)}, u32[]{:S(2)}, u32[]{:S(2)}) collective-permute-start(bf16[256,2048]{1,0:T(8,128)(2,1)} %collective-permute-done.3), channel_id=1, source_target_pairs={{0,8},{8,0},{16,24},{24,16},{1,9},{9,1},{17,25},{25,17},{2,10},{10... | collective-permute-start | bytes 3145736 | tf_op jit(solution)/shard_map/ppermute | solution.py:86
  157.1 3.7 %copy-start.3 = (bf16[256,2048]{1,0:T(8,128)(2,1)S(1)}, bf16[256,2048]{1,0:T(8,128)(2,1)}, u32[]{:S(2)}) copy-start(bf16[256,2048]{1,0:T(8,128)(2,1)} %param.13) | copy-start | bytes 3145732
  160.8 2.8 %copy-start.2 = (f32[192,2048]{1,0:T(8,128)S(1)}, f32[192,2048]{1,0:T(8,128)}, u32[]{:S(2)}) copy-start(f32[192,2048]{1,0:T(8,128)} %fusion.58) | copy-start | bytes 4718596
  165.2 1.9 %copy-start.1 = (f32[384,2048]{1,0:T(8,128)S(1)}, f32[384,2048]{1,0:T(8,128)}, u32[]{:S(2)}) copy-start(f32[384,2048]{1,0:T(8,128)} %fusion.32) | copy-start | bytes 9437188
